TPU v7x, 32 devices: a whole 2x2x4 slice. The times are simulated.
32 devices in a mesh: seq: 16 (over z, y, core), mp: 2 (over x).
Axes of the slice: x: 2, y: 2, z: 4, core: 2. Of those that a mesh axis runs over, the one named last changes fastest.
Arguments:
- tokens: bfloat16 [4096, 2048], P('seq'), may hold values from -25 to 25
- lengths: int32 [32], replicated, may hold values from 1 to 1024, 4096 in all
- prefix_cache: bfloat16 [4, 2048, 512], P(None, 'seq'), may hold values from -1000 to 1000
- attn_gain: bfloat16 [2048], replicated, may hold values from 0.25 to 1.75
- w_query: bfloat16 [2048, 2048], P(None, 'mp'), may hold values from -0.25 to 0.25
- w_keyval: bfloat16 [2048, 512], replicated, may hold values from -0.125 to 0.125
- w_out: bfloat16 [2048, 2048], P('mp'), may hold values from -0.25 to 0.25
- final_gain: bfloat16 [2048], replicated, may hold values from 0.25 to 1.75
- w_head: bfloat16 [2048, 32000], P(None, ('seq', 'mp')), may hold values from -0.4375 to 0.4375
Outputs:
- hidden: bfloat16 [4096, 2048], P('seq', 'mp')
- suffix_cache: bfloat16 [4096, 512], P('seq')
- last_normed: bfloat16 [32, 2048], replicated
- greatest: float32 [32], replicated
Inputs may be any that keep to these rules, and one draw needn't show every extreme that they name: The lengths sum to 4096 and one of them equals 1024.
All inputs are finite; a program needn't handle non-finite values.
Results may differ from a plain program's by a relative error of at most 0.013.
Values may be sent and summed in bfloat16 or wider, within the bound.
No kernel may reach another device: no remote copies, remote signals or barrier semaphores. Data moves between devices by JAX's collectives and lax.ppermute only.
A program may use at most 64 MiB of HBM per device.

v0:
```python
import math
import jax
import jax.numpy as jnp
from jax import lax
from jax.sharding import PartitionSpec as P

QH = 32
KVH = 4
HD = 64
G = 4
RPG = 8
P_SIZE = 2048
epsilon = 1e-05


def passed_along(block, axis, distance):
    devices = range(lax.axis_size(axis))
    route = [((i - distance) % len(devices), i) for i in devices]
    return lax.ppermute(block, axis, route)


def rotate(source, places, head_count):
    half_dim = HD // 2
    row_count = source.shape[0]
    reshaped = source.reshape(row_count, head_count, HD)
    frequency = 10000.0 ** (-(jnp.arange(half_dim, dtype=jnp.float32) * 2.0 / HD))
    angles = places.astype(jnp.float32)[:, None] * frequency[None, :]
    cos_table = jnp.cos(angles)[:, None, :]
    sine_table = jnp.sin(angles)[:, None, :]
    leading = reshaped[..., :half_dim]
    second = reshaped[..., half_dim:]
    joined = jnp.concatenate(
        [leading * cos_table - second * sine_table, second * cos_table + leading * sine_table], -1
    )
    return joined.reshape(row_count, head_count * HD)


def attend(running, queries, kv_block, allowed):
    old_max, old_sum, numerator = running
    half_width = kv_block.shape[1] // 2
    kv_heads = queries.shape[1]
    key_rows = kv_block[:, :half_width].reshape(kv_block.shape[0], kv_heads, HD)
    val_rows = kv_block[:, half_width:].reshape(kv_block.shape[0], kv_heads, HD)
    scores = jnp.einsum("qgrd,ngd->grqn", queries, key_rows, preferred_element_type=jnp.float32) * (
        1.0 / math.sqrt(HD)
    )
    scores = jnp.where(allowed[None, None], scores, -jnp.inf)
    new_max = jnp.maximum(old_max, jnp.max(scores, -1))
    factor = jnp.exp(old_max - new_max)
    weights = jnp.exp(scores - new_max[..., None])
    new_sum = old_sum * factor + jnp.sum(weights, -1)
    numerator = numerator * factor[..., None] + jnp.einsum(
        "grqn,ngd->grqd", weights.astype(jnp.bfloat16), val_rows, preferred_element_type=jnp.float32
    )
    return (new_max, new_sum, numerator)


def suffix_allowed(source_dev, token_rows, request, position, request_end):
    key_place = source_dev * token_rows + jnp.arange(token_rows, dtype=jnp.int32)
    key_request = jnp.sum((key_place[:, None] >= request_end[None, :]).astype(jnp.int32), 1)
    return (
        (request[:, None] == key_request[None, :])
        & (key_place[None, :] <= position[:, None])
        & (source_dev >= 0)
    )


def prefix_allowed(group_of, row_count):
    key_group = (
        jnp.arange(G, dtype=jnp.int32)[:, None] + jnp.zeros((1, row_count), jnp.int32)
    ).reshape(-1)
    return group_of[:, None] == key_group[None, :]


def per_device(
    tokens, lengths, prefix_cache, attn_gain, w_query, w_keyval, w_out, final_gain, w_head
):
    token_rows = tokens.shape[0]
    model_width = tokens.shape[1]
    seq_devices = lax.axis_size("seq")
    seq_index = lax.axis_index("seq")
    mp_index = lax.axis_index("mp")
    part_width = model_width // lax.axis_size("mp")
    query_heads = w_query.shape[1] // HD
    group_size = QH // KVH
    kv_heads = max(1, query_heads // group_size)
    repeat_count = query_heads // kv_heads
    kv_first = mp_index * query_heads // group_size
    kv_width = KVH * HD
    request_count = lengths.shape[0]
    activations = tokens.astype(jnp.float32)
    normed = (
        activations
        * lax.rsqrt(jnp.mean(activations * activations, -1, keepdims=True) + epsilon)
        * attn_gain.astype(jnp.float32)
    ).astype(jnp.bfloat16)
    request_end = jnp.cumsum(lengths)
    starts = request_end - lengths
    position = seq_index * token_rows + jnp.arange(token_rows, dtype=jnp.int32)
    request = jnp.sum((position[:, None] >= request_end[None, :]).astype(jnp.int32), 1)
    request_table = request[:, None] == jnp.arange(request_count, dtype=jnp.int32)[None, :]
    offset = position - jnp.sum(jnp.where(request_table, starts[None, :], 0), 1)
    group_of = request // RPG
    query_full = jnp.dot(normed, w_query, preferred_element_type=jnp.float32)
    keyval = jnp.dot(normed, w_keyval, preferred_element_type=jnp.float32)
    queries = (
        rotate(query_full, P_SIZE + offset, query_heads)
        .astype(jnp.bfloat16)
        .reshape(token_rows, kv_heads, repeat_count, HD)
    )
    key_rows = rotate(keyval[:, :kv_width], P_SIZE + offset, KVH).astype(jnp.bfloat16)
    val_rows = keyval[:, kv_width:].astype(jnp.bfloat16)
    suffix_cache = jnp.concatenate([key_rows, val_rows], 1)
    own_suffix = jnp.concatenate(
        [
            lax.dynamic_slice_in_dim(key_rows, kv_first * HD, kv_heads * HD, 1),
            lax.dynamic_slice_in_dim(val_rows, kv_first * HD, kv_heads * HD, 1),
        ],
        1,
    )
    own_prefix = jnp.concatenate(
        [
            lax.dynamic_slice_in_dim(prefix_cache, kv_first * HD, kv_heads * HD, 2),
            lax.dynamic_slice_in_dim(prefix_cache, kv_width + kv_first * HD, kv_heads * HD, 2),
        ],
        2,
    )
    prefix_rows = own_prefix.shape[1]
    block_width = own_prefix.shape[2]
    running = (
        jnp.full((kv_heads, repeat_count, token_rows), -1e30, jnp.float32),
        jnp.zeros((kv_heads, repeat_count, token_rows), jnp.float32),
        jnp.zeros((kv_heads, repeat_count, token_rows, HD), jnp.float32),
    )
    prefix_mask = prefix_allowed(group_of, prefix_rows)
    running = attend(
        running, queries, own_prefix.reshape(G * prefix_rows, block_width), prefix_mask
    )
    running = attend(
        running,
        queries,
        own_suffix,
        suffix_allowed(seq_index, token_rows, request, position, request_end),
    )

    def cycle_hop(hop_count, loop_state):
        state_now, prefix_block, suffix_block = loop_state
        prefix_block, suffix_block = passed_along((prefix_block, suffix_block), "seq", 1)
        source_dev = (seq_index - hop_count) % seq_devices
        state_now = attend(
            state_now, queries, prefix_block.reshape(G * prefix_rows, block_width), prefix_mask
        )
        state_now = attend(
            state_now,
            queries,
            suffix_block,
            suffix_allowed(source_dev, token_rows, request, position, request_end),
        )
        return (state_now, prefix_block, suffix_block)

    running, unused_prefix, unused_suffix = lax.fori_loop(
        1, seq_devices, cycle_hop, (running, own_prefix, own_suffix)
    )
    final_max, final_sum, numerator = running
    context = numerator / final_sum[..., None]
    context = (
        jnp.transpose(context, (2, 0, 1, 3))
        .reshape(token_rows, query_heads * HD)
        .astype(jnp.bfloat16)
    )
    mixture = jnp.dot(context, w_out, preferred_element_type=jnp.float32)
    mixture = lax.psum_scatter(
        mixture.astype(jnp.bfloat16), "mp", scatter_dimension=1, tiled=True
    ).astype(jnp.float32)
    own_columns = lax.dynamic_slice_in_dim(activations, mp_index * part_width, part_width, 1)
    hidden = (own_columns + mixture).astype(jnp.bfloat16)
    local_last = request_end - 1 - seq_index * token_rows
    onehot = (local_last[:, None] == jnp.arange(token_rows, dtype=jnp.int32)[None, :]).astype(
        jnp.bfloat16
    )
    last_part = jnp.dot(onehot, hidden, preferred_element_type=jnp.float32)
    canvas = lax.dynamic_update_slice_in_dim(
        jnp.zeros((request_count, model_width), jnp.float32), last_part, mp_index * part_width, 1
    )
    last_rows = lax.psum(canvas, ("seq", "mp"))
    inv_rms = lax.rsqrt(jnp.mean(last_rows * last_rows, -1, keepdims=True) + epsilon)
    last_normed = (last_rows * final_gain.astype(jnp.float32) * inv_rms).astype(jnp.bfloat16)
    logits = jnp.dot(last_normed, w_head, preferred_element_type=jnp.float32)
    greatest = lax.pmax(jnp.max(logits, -1), ("seq", "mp"))
    return (hidden, suffix_cache, last_normed, greatest)


def solution(mesh):
    return jax.shard_map(
        per_device,
        mesh=mesh,
        in_specs=(
            P("seq", None),
            P(),
            P(None, "seq", None),
            P(),
            P(None, "mp"),
            P(),
            P("mp", None),
            P(),
            P(None, ("seq", "mp")),
        ),
        out_specs=(P("seq", "mp"), P("seq", None), P(), P()),
        check_vma=False,
    )
```

profile of v0, /device:TPU:0, one launch (start us, length us, event | category | flops | bytes accessed | tf_op | source)
XLA Modules:
  0.0 527.1 jit_solution(17378786312400722219)
XLA Ops:
  20.0 4.0 fusion.51
  33.5 2.3 fusion.47
  38.0 280.5 %while.24 = (s32[]{:T(128)}, f32[2,8,256]{2,1,0:T(8,128)S(1)}, f32[2,8,256]{2,1,0:T(8,128)S(1)}, f32[2,8,256,64]{2,3,1,0:T(8,128)}, bf16[4,128,256]{1,0,2:T(4,12...) while((s32[]{:T(128)}, f32[2,8,256]{2,1,0:T(8,128)S(1)}, ...), condition=%wide.region_14.15_spmd.clone, body=%wide.region_8.14_spmd.clone.sunk | while | flops 841392384 | bytes 52473384 | solution.py:161
  38.5 2.6 collective-permute-start.1
  41.6 4.6 collective-permute-done
  58.2 6.6 %collective-permute-done = bf16[256,256]{0,1:T(8,128)(2,1)S(1)} collective-permute-done((bf16[256,256]{0,1:T(8,128)(2,1)S(1)}, bf16[256,256]{0,1:T(8,128)(2,1)S(1)}, u32[]{:S(2)}, u32[]{:S(2)}) %collective-permute-start) | collective-permute-done | bytes 131104 | tf_op jit(solution)/shard_map/while/body/eval_jaxpr/ppermute | solution.py:19
  76.9 6.6 %collective-permute-done = bf16[256,256]{0,1:T(8,128)(2,1)S(1)} collective-permute-done((bf16[256,256]{0,1:T(8,128)(2,1)S(1)}, bf16[256,256]{0,1:T(8,128)(2,1)S(1)}, u32[]{:S(2)}, u32[]{:S(2)}) %collective-permute-start) | collective-permute-done | bytes 131104 | tf_op jit(solution)/shard_map/while/body/eval_jaxpr/ppermute | solution.py:19
  95.5 6.6 %collective-permute-done = bf16[256,256]{0,1:T(8,128)(2,1)S(1)} collective-permute-done((bf16[256,256]{0,1:T(8,128)(2,1)S(1)}, bf16[256,256]{0,1:T(8,128)(2,1)S(1)}, u32[]{:S(2)}, u32[]{:S(2)}) %collective-permute-start) | collective-permute-done | bytes 131104 | tf_op jit(solution)/shard_map/while/body/eval_jaxpr/ppermute | solution.py:19
  114.1 6.6 %collective-permute-done = bf16[256,256]{0,1:T(8,128)(2,1)S(1)} collective-permute-done((bf16[256,256]{0,1:T(8,128)(2,1)S(1)}, bf16[256,256]{0,1:T(8,128)(2,1)S(1)}, u32[]{:S(2)}, u32[]{:S(2)}) %collective-permute-start) | collective-permute-done | bytes 131104 | tf_op jit(solution)/shard_map/while/body/eval_jaxpr/ppermute | solution.py:19
  132.8 6.6 %collective-permute-done = bf16[256,256]{0,1:T(8,128)(2,1)S(1)} collective-permute-done((bf16[256,256]{0,1:T(8,128)(2,1)S(1)}, bf16[256,256]{0,1:T(8,128)(2,1)S(1)}, u32[]{:S(2)}, u32[]{:S(2)}) %collective-permute-start) | collective-permute-done | bytes 131104 | tf_op jit(solution)/shard_map/while/body/eval_jaxpr/ppermute | solution.py:19
  151.4 6.6 %collective-permute-done = bf16[256,256]{0,1:T(8,128)(2,1)S(1)} collective-permute-done((bf16[256,256]{0,1:T(8,128)(2,1)S(1)}, bf16[256,256]{0,1:T(8,128)(2,1)S(1)}, u32[]{:S(2)}, u32[]{:S(2)}) %collective-permute-start) | collective-permute-done | bytes 131104 | tf_op jit(solution)/shard_map/while/body/eval_jaxpr/ppermute | solution.py:19
  170.0 6.6 %collective-permute-done = bf16[256,256]{0,1:T(8,128)(2,1)S(1)} collective-permute-done((bf16[256,256]{0,1:T(8,128)(2,1)S(1)}, bf16[256,256]{0,1:T(8,128)(2,1)S(1)}, u32[]{:S(2)}, u32[]{:S(2)}) %collective-permute-start) | collective-permute-done | bytes 131104 | tf_op jit(solution)/shard_map/while/body/eval_jaxpr/ppermute | solution.py:19
  188.7 6.6 %collective-permute-done = bf16[256,256]{0,1:T(8,128)(2,1)S(1)} collective-permute-done((bf16[256,256]{0,1:T(8,128)(2,1)S(1)}, bf16[256,256]{0,1:T(8,128)(2,1)S(1)}, u32[]{:S(2)}, u32[]{:S(2)}) %collective-permute-start) | collective-permute-done | bytes 131104 | tf_op jit(solution)/shard_map/while/body/eval_jaxpr/ppermute | solution.py:19
  207.3 6.6 %collective-permute-done = bf16[256,256]{0,1:T(8,128)(2,1)S(1)} collective-permute-done((bf16[256,256]{0,1:T(8,128)(2,1)S(1)}, bf16[256,256]{0,1:T(8,128)(2,1)S(1)}, u32[]{:S(2)}, u32[]{:S(2)}) %collective-permute-start) | collective-permute-done | bytes 131104 | tf_op jit(solution)/shard_map/while/body/eval_jaxpr/ppermute | solution.py:19
  225.9 6.6 %collective-permute-done = bf16[256,256]{0,1:T(8,128)(2,1)S(1)} collective-permute-done((bf16[256,256]{0,1:T(8,128)(2,1)S(1)}, bf16[256,256]{0,1:T(8,128)(2,1)S(1)}, u32[]{:S(2)}, u32[]{:S(2)}) %collective-permute-start) | collective-permute-done | bytes 131104 | tf_op jit(solution)/shard_map/while/body/eval_jaxpr/ppermute | solution.py:19
  244.6 6.6 %collective-permute-done = bf16[256,256]{0,1:T(8,128)(2,1)S(1)} collective-permute-done((bf16[256,256]{0,1:T(8,128)(2,1)S(1)}, bf16[256,256]{0,1:T(8,128)(2,1)S(1)}, u32[]{:S(2)}, u32[]{:S(2)}) %collective-permute-start) | collective-permute-done | bytes 131104 | tf_op jit(solution)/shard_map/while/body/eval_jaxpr/ppermute | solution.py:19
  263.2 6.6 %collective-permute-done = bf16[256,256]{0,1:T(8,128)(2,1)S(1)} collective-permute-done((bf16[256,256]{0,1:T(8,128)(2,1)S(1)}, bf16[256,256]{0,1:T(8,128)(2,1)S(1)}, u32[]{:S(2)}, u32[]{:S(2)}) %collective-permute-start) | collective-permute-done | bytes 131104 | tf_op jit(solution)/shard_map/while/body/eval_jaxpr/ppermute | solution.py:19
  281.9 6.6 %collective-permute-done = bf16[256,256]{0,1:T(8,128)(2,1)S(1)} collective-permute-done((bf16[256,256]{0,1:T(8,128)(2,1)S(1)}, bf16[256,256]{0,1:T(8,128)(2,1)S(1)}, u32[]{:S(2)}, u32[]{:S(2)}) %collective-permute-start) | collective-permute-done | bytes 131104 | tf_op jit(solution)/shard_map/while/body/eval_jaxpr/ppermute | solution.py:19
  300.5 6.6 %collective-permute-done = bf16[256,256]{0,1:T(8,128)(2,1)S(1)} collective-permute-done((bf16[256,256]{0,1:T(8,128)(2,1)S(1)}, bf16[256,256]{0,1:T(8,128)(2,1)S(1)}, u32[]{:S(2)}, u32[]{:S(2)}) %collective-permute-start) | collective-permute-done | bytes 131104 | tf_op jit(solution)/shard_map/while/body/eval_jaxpr/ppermute | solution.py:19
  319.9 4.5 convolution_convert_fusion
  326.1 16.5 %reduce-scatter.2.cloned.1.call-done = bf16[256,1024]{1,0:T(8,128)(2,1)} async-done(((bf16[256,2048]{1,0:T(8,128)(2,1)}), bf16[256,1024]{1,0:T(8,128)(2,1)}) %reduce-scatter.2.cloned.1.call-update) | async-done | bytes 524304 | tf_op jit(solution)/shard_map/reduce_scatter | solution.py:172
  345.2 129.4 %all-reduce.2.cloned.1.call-done = f32[32,2048]{1,0:T(8,128)} async-done(((f32[32,2048]{1,0:T(8,128)}), f32[32,2048]{1,0:T(8,128)}) %all-reduce.2.cloned.1.call-update) | async-done | bytes 262160 | tf_op jit(solution)/shard_map/psum | solution.py:185
  476.7 3.6 convolution_reduce_fusion
  481.1 39.2 %pmax.7 = f32[32]{0:T(128)} all-reduce(f32[32]{0:T(128)S(1)} %convolution_reduce_fusion), channel_id=1, replica_groups=mesh['seq'=16,'mp'=2] {'seq','mp'}, use_global_device_ids=true, to_apply=%region_19.20 | all-reduce | flops 32 | bytes 256 | tf_op jit(solution)/shard_map/pmax | solution.py:189
  (483 shorter events, 211.0 us)
Async XLA Ops:
  7.2 335.4 %reduce-scatter.2.cloned.1.call-start = ((), (), s32[]{:S(2)}) async-start(), calls=%async_computation.1 | async-start | bytes 1572864 | tf_op jit(solution)/shard_map/reduce_scatter | solution.py:172
  38.0 8.1 %collective-permute-start = (bf16[256,256]{0,1:T(8,128)(2,1)S(1)}, bf16[256,256]{0,1:T(8,128)(2,1)S(1)}, u32[]{:S(2)}, u32[]{:S(2)}) collective-permute-start(bf16[256,256]{0,1:T(8,128)(2,1)S(1)} %get-tuple-element.555), channel_id=1, source_target_pairs={{30,0},{0,2},{2,4},{4,6},{6,8},{8,10},{10,12},{12,14},{14,16},{16,... | collective-permute-start | bytes 393224 | tf_op jit(solution)/shard_map/while/body/eval_jaxpr/ppermute | solution.py:19
  38.5 10.4 %collective-permute-start.1 = (bf16[4,128,256]{1,0,2:T(4,128)(2,1)S(1)}, bf16[4,128,256]{1,0,2:T(4,128)(2,1)S(1)}, u32[]{:S(2)}, u32[]{:S(2)}) collective-permute-start(bf16[4,128,256]{1,0,2:T(4,128)(2,1)S(1)} %get-tuple-element.554), channel_id=1, source_target_pairs={{30,0},{0,2},{2,4},{4,6},{6,8},{8,10},{10,12},{12,14},{14,16},{16,... | collective-permute-start | bytes 786440 | tf_op jit(solution)/shard_map/while/body/eval_jaxpr/ppermute | solution.py:19
  57.7 7.1 %collective-permute-start = (bf16[256,256]{0,1:T(8,128)(2,1)S(1)}, bf16[256,256]{0,1:T(8,128)(2,1)S(1)}, u32[]{:S(2)}, u32[]{:S(2)}) collective-permute-start(bf16[256,256]{0,1:T(8,128)(2,1)S(1)} %get-tuple-element.555), channel_id=1, source_target_pairs={{30,0},{0,2},{2,4},{4,6},{6,8},{8,10},{10,12},{12,14},{14,16},{16,... | collective-permute-start | bytes 393224 | tf_op jit(solution)/shard_map/while/body/eval_jaxpr/ppermute | solution.py:19
  57.7 9.9 %collective-permute-start.1 = (bf16[4,128,256]{1,0,2:T(4,128)(2,1)S(1)}, bf16[4,128,256]{1,0,2:T(4,128)(2,1)S(1)}, u32[]{:S(2)}, u32[]{:S(2)}) collective-permute-start(bf16[4,128,256]{1,0,2:T(4,128)(2,1)S(1)} %get-tuple-element.554), channel_id=1, source_target_pairs={{30,0},{0,2},{2,4},{4,6},{6,8},{8,10},{10,12},{12,14},{14,16},{16,... | collective-permute-start | bytes 786440 | tf_op jit(solution)/shard_map/while/body/eval_jaxpr/ppermute | solution.py:19
  76.3 7.1 %collective-permute-start = (bf16[256,256]{0,1:T(8,128)(2,1)S(1)}, bf16[256,256]{0,1:T(8,128)(2,1)S(1)}, u32[]{:S(2)}, u32[]{:S(2)}) collective-permute-start(bf16[256,256]{0,1:T(8,128)(2,1)S(1)} %get-tuple-element.555), channel_id=1, source_target_pairs={{30,0},{0,2},{2,4},{4,6},{6,8},{8,10},{10,12},{12,14},{14,16},{16,... | collective-permute-start | bytes 393224 | tf_op jit(solution)/shard_map/while/body/eval_jaxpr/ppermute | solution.py:19
  76.4 9.9 %collective-permute-start.1 = (bf16[4,128,256]{1,0,2:T(4,128)(2,1)S(1)}, bf16[4,128,256]{1,0,2:T(4,128)(2,1)S(1)}, u32[]{:S(2)}, u32[]{:S(2)}) collective-permute-start(bf16[4,128,256]{1,0,2:T(4,128)(2,1)S(1)} %get-tuple-element.554), channel_id=1, source_target_pairs={{30,0},{0,2},{2,4},{4,6},{6,8},{8,10},{10,12},{12,14},{14,16},{16,... | collective-permute-start | bytes 786440 | tf_op jit(solution)/shard_map/while/body/eval_jaxpr/ppermute | solution.py:19
  95.0 9.9 %collective-permute-start.1 = (bf16[4,128,256]{1,0,2:T(4,128)(2,1)S(1)}, bf16[4,128,256]{1,0,2:T(4,128)(2,1)S(1)}, u32[]{:S(2)}, u32[]{:S(2)}) collective-permute-start(bf16[4,128,256]{1,0,2:T(4,128)(2,1)S(1)} %get-tuple-element.554), channel_id=1, source_target_pairs={{30,0},{0,2},{2,4},{4,6},{6,8},{8,10},{10,12},{12,14},{14,16},{16,... | collective-permute-start | bytes 786440 | tf_op jit(solution)/shard_map/while/body/eval_jaxpr/ppermute | solution.py:19
  113.6 7.1 %collective-permute-start = (bf16[256,256]{0,1:T(8,128)(2,1)S(1)}, bf16[256,256]{0,1:T(8,128)(2,1)S(1)}, u32[]{:S(2)}, u32[]{:S(2)}) collective-permute-start(bf16[256,256]{0,1:T(8,128)(2,1)S(1)} %get-tuple-element.555), channel_id=1, source_target_pairs={{30,0},{0,2},{2,4},{4,6},{6,8},{8,10},{10,12},{12,14},{14,16},{16,... | collective-permute-start | bytes 393224 | tf_op jit(solution)/shard_map/while/body/eval_jaxpr/ppermute | solution.py:19
  113.6 9.9 %collective-permute-start.1 = (bf16[4,128,256]{1,0,2:T(4,128)(2,1)S(1)}, bf16[4,128,256]{1,0,2:T(4,128)(2,1)S(1)}, u32[]{:S(2)}, u32[]{:S(2)}) collective-permute-start(bf16[4,128,256]{1,0,2:T(4,128)(2,1)S(1)} %get-tuple-element.554), channel_id=1, source_target_pairs={{30,0},{0,2},{2,4},{4,6},{6,8},{8,10},{10,12},{12,14},{14,16},{16,... | collective-permute-start | bytes 786440 | tf_op jit(solution)/shard_map/while/body/eval_jaxpr/ppermute | solution.py:19
  132.3 9.9 %collective-permute-start.1 = (bf16[4,128,256]{1,0,2:T(4,128)(2,1)S(1)}, bf16[4,128,256]{1,0,2:T(4,128)(2,1)S(1)}, u32[]{:S(2)}, u32[]{:S(2)}) collective-permute-start(bf16[4,128,256]{1,0,2:T(4,128)(2,1)S(1)} %get-tuple-element.554), channel_id=1, source_target_pairs={{30,0},{0,2},{2,4},{4,6},{6,8},{8,10},{10,12},{12,14},{14,16},{16,... | collective-permute-start | bytes 786440 | tf_op jit(solution)/shard_map/while/body/eval_jaxpr/ppermute | solution.py:19
  150.8 7.1 %collective-permute-start = (bf16[256,256]{0,1:T(8,128)(2,1)S(1)}, bf16[256,256]{0,1:T(8,128)(2,1)S(1)}, u32[]{:S(2)}, u32[]{:S(2)}) collective-permute-start(bf16[256,256]{0,1:T(8,128)(2,1)S(1)} %get-tuple-element.555), channel_id=1, source_target_pairs={{30,0},{0,2},{2,4},{4,6},{6,8},{8,10},{10,12},{12,14},{14,16},{16,... | collective-permute-start | bytes 393224 | tf_op jit(solution)/shard_map/while/body/eval_jaxpr/ppermute | solution.py:19
  150.9 9.9 %collective-permute-start.1 = (bf16[4,128,256]{1,0,2:T(4,128)(2,1)S(1)}, bf16[4,128,256]{1,0,2:T(4,128)(2,1)S(1)}, u32[]{:S(2)}, u32[]{:S(2)}) collective-permute-start(bf16[4,128,256]{1,0,2:T(4,128)(2,1)S(1)} %get-tuple-element.554), channel_id=1, source_target_pairs={{30,0},{0,2},{2,4},{4,6},{6,8},{8,10},{10,12},{12,14},{14,16},{16,... | collective-permute-start | bytes 786440 | tf_op jit(solution)/shard_map/while/body/eval_jaxpr/ppermute | solution.py:19
  169.5 9.9 %collective-permute-start.1 = (bf16[4,128,256]{1,0,2:T(4,128)(2,1)S(1)}, bf16[4,128,256]{1,0,2:T(4,128)(2,1)S(1)}, u32[]{:S(2)}, u32[]{:S(2)}) collective-permute-start(bf16[4,128,256]{1,0,2:T(4,128)(2,1)S(1)} %get-tuple-element.554), channel_id=1, source_target_pairs={{30,0},{0,2},{2,4},{4,6},{6,8},{8,10},{10,12},{12,14},{14,16},{16,... | collective-permute-start | bytes 786440 | tf_op jit(solution)/shard_map/while/body/eval_jaxpr/ppermute | solution.py:19
  188.1 7.1 %collective-permute-start = (bf16[256,256]{0,1:T(8,128)(2,1)S(1)}, bf16[256,256]{0,1:T(8,128)(2,1)S(1)}, u32[]{:S(2)}, u32[]{:S(2)}) collective-permute-start(bf16[256,256]{0,1:T(8,128)(2,1)S(1)} %get-tuple-element.555), channel_id=1, source_target_pairs={{30,0},{0,2},{2,4},{4,6},{6,8},{8,10},{10,12},{12,14},{14,16},{16,... | collective-permute-start | bytes 393224 | tf_op jit(solution)/shard_map/while/body/eval_jaxpr/ppermute | solution.py:19
  188.2 9.9 %collective-permute-start.1 = (bf16[4,128,256]{1,0,2:T(4,128)(2,1)S(1)}, bf16[4,128,256]{1,0,2:T(4,128)(2,1)S(1)}, u32[]{:S(2)}, u32[]{:S(2)}) collective-permute-start(bf16[4,128,256]{1,0,2:T(4,128)(2,1)S(1)} %get-tuple-element.554), channel_id=1, source_target_pairs={{30,0},{0,2},{2,4},{4,6},{6,8},{8,10},{10,12},{12,14},{14,16},{16,... | collective-permute-start | bytes 786440 | tf_op jit(solution)/shard_map/while/body/eval_jaxpr/ppermute | solution.py:19
  206.8 9.9 %collective-permute-start.1 = (bf16[4,128,256]{1,0,2:T(4,128)(2,1)S(1)}, bf16[4,128,256]{1,0,2:T(4,128)(2,1)S(1)}, u32[]{:S(2)}, u32[]{:S(2)}) collective-permute-start(bf16[4,128,256]{1,0,2:T(4,128)(2,1)S(1)} %get-tuple-element.554), channel_id=1, source_target_pairs={{30,0},{0,2},{2,4},{4,6},{6,8},{8,10},{10,12},{12,14},{14,16},{16,... | collective-permute-start | bytes 786440 | tf_op jit(solution)/shard_map/while/body/eval_jaxpr/ppermute | solution.py:19
  225.4 7.1 %collective-permute-start = (bf16[256,256]{0,1:T(8,128)(2,1)S(1)}, bf16[256,256]{0,1:T(8,128)(2,1)S(1)}, u32[]{:S(2)}, u32[]{:S(2)}) collective-permute-start(bf16[256,256]{0,1:T(8,128)(2,1)S(1)} %get-tuple-element.555), channel_id=1, source_target_pairs={{30,0},{0,2},{2,4},{4,6},{6,8},{8,10},{10,12},{12,14},{14,16},{16,... | collective-permute-start | bytes 393224 | tf_op jit(solution)/shard_map/while/body/eval_jaxpr/ppermute | solution.py:19
  225.4 9.9 %collective-permute-start.1 = (bf16[4,128,256]{1,0,2:T(4,128)(2,1)S(1)}, bf16[4,128,256]{1,0,2:T(4,128)(2,1)S(1)}, u32[]{:S(2)}, u32[]{:S(2)}) collective-permute-start(bf16[4,128,256]{1,0,2:T(4,128)(2,1)S(1)} %get-tuple-element.554), channel_id=1, source_target_pairs={{30,0},{0,2},{2,4},{4,6},{6,8},{8,10},{10,12},{12,14},{14,16},{16,... | collective-permute-start | bytes 786440 | tf_op jit(solution)/shard_map/while/body/eval_jaxpr/ppermute | solution.py:19
  244.1 9.9 %collective-permute-start.1 = (bf16[4,128,256]{1,0,2:T(4,128)(2,1)S(1)}, bf16[4,128,256]{1,0,2:T(4,128)(2,1)S(1)}, u32[]{:S(2)}, u32[]{:S(2)}) collective-permute-start(bf16[4,128,256]{1,0,2:T(4,128)(2,1)S(1)} %get-tuple-element.554), channel_id=1, source_target_pairs={{30,0},{0,2},{2,4},{4,6},{6,8},{8,10},{10,12},{12,14},{14,16},{16,... | collective-permute-start | bytes 786440 | tf_op jit(solution)/shard_map/while/body/eval_jaxpr/ppermute | solution.py:19
  262.7 9.9 %collective-permute-start.1 = (bf16[4,128,256]{1,0,2:T(4,128)(2,1)S(1)}, bf16[4,128,256]{1,0,2:T(4,128)(2,1)S(1)}, u32[]{:S(2)}, u32[]{:S(2)}) collective-permute-start(bf16[4,128,256]{1,0,2:T(4,128)(2,1)S(1)} %get-tuple-element.554), channel_id=1, source_target_pairs={{30,0},{0,2},{2,4},{4,6},{6,8},{8,10},{10,12},{12,14},{14,16},{16,... | collective-permute-start | bytes 786440 | tf_op jit(solution)/shard_map/while/body/eval_jaxpr/ppermute | solution.py:19
  281.4 9.9 %collective-permute-start.1 = (bf16[4,128,256]{1,0,2:T(4,128)(2,1)S(1)}, bf16[4,128,256]{1,0,2:T(4,128)(2,1)S(1)}, u32[]{:S(2)}, u32[]{:S(2)}) collective-permute-start(bf16[4,128,256]{1,0,2:T(4,128)(2,1)S(1)} %get-tuple-element.554), channel_id=1, source_target_pairs={{30,0},{0,2},{2,4},{4,6},{6,8},{8,10},{10,12},{12,14},{14,16},{16,... | collective-permute-start | bytes 786440 | tf_op jit(solution)/shard_map/while/body/eval_jaxpr/ppermute | solution.py:19
  300.0 9.9 %collective-permute-start.1 = (bf16[4,128,256]{1,0,2:T(4,128)(2,1)S(1)}, bf16[4,128,256]{1,0,2:T(4,128)(2,1)S(1)}, u32[]{:S(2)}, u32[]{:S(2)}) collective-permute-start(bf16[4,128,256]{1,0,2:T(4,128)(2,1)S(1)} %get-tuple-element.554), channel_id=1, source_target_pairs={{30,0},{0,2},{2,4},{4,6},{6,8},{8,10},{10,12},{12,14},{14,16},{16,... | collective-permute-start | bytes 786440 | tf_op jit(solution)/shard_map/while/body/eval_jaxpr/ppermute | solution.py:19
  324.5 150.1 %all-reduce.2.cloned.1.call-start = ((), (), s32[]{:S(2)}) async-start(), calls=%async_computation.2 | async-start | bytes 524288 | tf_op jit(solution)/shard_map/psum | solution.py:185
  (56 other events, 733.8 us)
Sparse Core Ops, SparseCore 0:
  324.6 17.9 reduce-scatter.1
  349.6 124.9 all-reduce.1
where the time goes:
time: 528 us; the launch traced here: 527 us
  waiting for transfers between devices  272 us (52%)
  matrix products  117 us (22%)
  other arithmetic  60.6 us (11%)
  blocking collectives  39.2 us (7%)
  local copies, waits for them, and re-layouts  15.9 us (3%)
  between operations  14.7 us (3%)
    psum x1, waiting for transfers between devices, per_device(): last_rows = lax.psum(canvas, ('seq', 'mp'))  129 us
    ppermute x30, waiting for transfers between devices, passed_along(): return lax.ppermute(block, axis, route)  126 us
    dot_general x32, matrix products, attend(): jnp.einsum('grqn,ngd->grqd', weights.astype(jnp.bfloat16), val_rows, pref...  67.5 us
    reduce_sum x32, other arithmetic, attend(): new_sum = old_sum * factor + jnp.sum(weights, -1)  40.8 us
    pmax x1, blocking collectives, per_device(): greatest = lax.pmax(jnp.max(logits, -1), ('seq', 'mp'))  39.2 us
    dot_general x32, matrix products, attend(): jnp.einsum('qgrd,ngd->grqn', queries, key_rows, preferred_element_type=jn...  35.1 us
    reduce_scatter x1, waiting for transfers between devices, per_device(): lax.psum_scatter(mixture.astype(jnp.bfloat16), 'mp', scatter_dimension=1,...  16.5 us
  transfers between devices with their start and end apart: 32, of which 32 were waited for; matrix products, arithmetic and copies ran while one was open for 4% of the time, Pallas kernels for 0%

commit v1 on v0

--- a/solution.py
+++ b/solution.py
@@ -182,7 +182,7 @@
     canvas = lax.dynamic_update_slice_in_dim(
         jnp.zeros((request_count, model_width), jnp.float32), last_part, mp_index * part_width, 1
     )
-    last_rows = lax.psum(canvas, ("seq", "mp"))
+    last_rows = lax.all_gather(canvas, ("seq", "mp")).sum(axis=0)
     inv_rms = lax.rsqrt(jnp.mean(last_rows * last_rows, -1, keepdims=True) + epsilon)
     last_normed = (last_rows * final_gain.astype(jnp.float32) * inv_rms).astype(jnp.bfloat16)
     logits = jnp.dot(last_normed, w_head, preferred_element_type=jnp.float32)

time: 528 us -> 482 us (0.913)
  waiting for transfers between devices: 272 us -> 222 us
    psum x1 -> x0, waiting for transfers between devices: 129 us -> none  [per_device(): last_rows = lax.psum(canvas, ('seq', 'mp'))]
    all_gather x0 -> x1, waiting for transfers between devices: none -> 78.9 us  [per_device(): last_rows = lax.all_gather(canvas, ('seq', 'mp')).sum(axis=0)]
where the time goes in v1:
time: 482 us; the launch traced here: 481 us
  waiting for transfers between devices  222 us (46%)
  matrix products  117 us (24%)
  other arithmetic  65 us (13%)
  blocking collectives  39.2 us (8%)
  local copies, waits for them, and re-layouts  15.9 us (3%)
  between operations  14.6 us (3%)
  starting transfers between devices  5.05 us (1%)
    ppermute x30, waiting for transfers between devices, passed_along(): return lax.ppermute(block, axis, route)  126 us
    all_gather x1, waiting for transfers between devices, per_device(): last_rows = lax.all_gather(canvas, ('seq', 'mp')).sum(axis=0)  78.9 us
    dot_general x32, matrix products, attend(): jnp.einsum('grqn,ngd->grqd', weights.astype(jnp.bfloat16), val_rows, pref...  67.8 us
    reduce_sum x32, other arithmetic, attend(): new_sum = old_sum * factor + jnp.sum(weights, -1)  40.8 us
    pmax x1, blocking collectives, per_device(): greatest = lax.pmax(jnp.max(logits, -1), ('seq', 'mp'))  39.2 us
    dot_general x32, matrix products, attend(): jnp.einsum('qgrd,ngd->grqn', queries, key_rows, preferred_element_type=jn...  35 us
    reduce_scatter x1, waiting for transfers between devices, per_device(): lax.psum_scatter(mixture.astype(jnp.bfloat16), 'mp', scatter_dimension=1,...  16.3 us
  transfers between devices with their start and end apart: 32, of which 32 were waited for; matrix products, arithmetic and copies ran while one was open for 4% of the time, Pallas kernels for 0%

profile of v1, /device:TPU:0, one launch (start us, length us, event | category | flops | bytes accessed | tf_op | source)
XLA Modules:
  0.0 481.1 jit_solution(15878601705479982073)
XLA Ops:
  20.2 4.0 fusion.52
  40.4 280.8 %while.24 = (s32[]{:T(128)}, f32[2,8,256]{2,1,0:T(8,128)S(1)}, f32[2,8,256]{2,1,0:T(8,128)S(1)}, f32[2,8,256,64]{2,3,1,0:T(8,128)}, bf16[4,128,256]{1,0,2:T(4,12...) while((s32[]{:T(128)}, f32[2,8,256]{2,1,0:T(8,128)S(1)}, ...), condition=%wide.region_14.15_spmd.clone, body=%wide.region_8.14_spmd.clone.sunk | while | flops 841392384 | bytes 52473384 | solution.py:161
  40.9 2.6 collective-permute-start.1
  43.9 4.6 collective-permute-done
  60.6 6.6 %collective-permute-done = bf16[256,256]{0,1:T(8,128)(2,1)S(1)} collective-permute-done((bf16[256,256]{0,1:T(8,128)(2,1)S(1)}, bf16[256,256]{0,1:T(8,128)(2,1)S(1)}, u32[]{:S(2)}, u32[]{:S(2)}) %collective-permute-start) | collective-permute-done | bytes 131104 | tf_op jit(solution)/shard_map/while/body/eval_jaxpr/ppermute | solution.py:19
  79.2 6.6 %collective-permute-done = bf16[256,256]{0,1:T(8,128)(2,1)S(1)} collective-permute-done((bf16[256,256]{0,1:T(8,128)(2,1)S(1)}, bf16[256,256]{0,1:T(8,128)(2,1)S(1)}, u32[]{:S(2)}, u32[]{:S(2)}) %collective-permute-start) | collective-permute-done | bytes 131104 | tf_op jit(solution)/shard_map/while/body/eval_jaxpr/ppermute | solution.py:19
  97.9 6.6 %collective-permute-done = bf16[256,256]{0,1:T(8,128)(2,1)S(1)} collective-permute-done((bf16[256,256]{0,1:T(8,128)(2,1)S(1)}, bf16[256,256]{0,1:T(8,128)(2,1)S(1)}, u32[]{:S(2)}, u32[]{:S(2)}) %collective-permute-start) | collective-permute-done | bytes 131104 | tf_op jit(solution)/shard_map/while/body/eval_jaxpr/ppermute | solution.py:19
  116.6 6.6 %collective-permute-done = bf16[256,256]{0,1:T(8,128)(2,1)S(1)} collective-permute-done((bf16[256,256]{0,1:T(8,128)(2,1)S(1)}, bf16[256,256]{0,1:T(8,128)(2,1)S(1)}, u32[]{:S(2)}, u32[]{:S(2)}) %collective-permute-start) | collective-permute-done | bytes 131104 | tf_op jit(solution)/shard_map/while/body/eval_jaxpr/ppermute | solution.py:19
  135.2 6.6 %collective-permute-done = bf16[256,256]{0,1:T(8,128)(2,1)S(1)} collective-permute-done((bf16[256,256]{0,1:T(8,128)(2,1)S(1)}, bf16[256,256]{0,1:T(8,128)(2,1)S(1)}, u32[]{:S(2)}, u32[]{:S(2)}) %collective-permute-start) | collective-permute-done | bytes 131104 | tf_op jit(solution)/shard_map/while/body/eval_jaxpr/ppermute | solution.py:19
  153.9 6.6 %collective-permute-done = bf16[256,256]{0,1:T(8,128)(2,1)S(1)} collective-permute-done((bf16[256,256]{0,1:T(8,128)(2,1)S(1)}, bf16[256,256]{0,1:T(8,128)(2,1)S(1)}, u32[]{:S(2)}, u32[]{:S(2)}) %collective-permute-start) | collective-permute-done | bytes 131104 | tf_op jit(solution)/shard_map/while/body/eval_jaxpr/ppermute | solution.py:19
  172.5 6.6 %collective-permute-done = bf16[256,256]{0,1:T(8,128)(2,1)S(1)} collective-permute-done((bf16[256,256]{0,1:T(8,128)(2,1)S(1)}, bf16[256,256]{0,1:T(8,128)(2,1)S(1)}, u32[]{:S(2)}, u32[]{:S(2)}) %collective-permute-start) | collective-permute-done | bytes 131104 | tf_op jit(solution)/shard_map/while/body/eval_jaxpr/ppermute | solution.py:19
  191.2 6.6 %collective-permute-done = bf16[256,256]{0,1:T(8,128)(2,1)S(1)} collective-permute-done((bf16[256,256]{0,1:T(8,128)(2,1)S(1)}, bf16[256,256]{0,1:T(8,128)(2,1)S(1)}, u32[]{:S(2)}, u32[]{:S(2)}) %collective-permute-start) | collective-permute-done | bytes 131104 | tf_op jit(solution)/shard_map/while/body/eval_jaxpr/ppermute | solution.py:19
  209.8 6.6 %collective-permute-done = bf16[256,256]{0,1:T(8,128)(2,1)S(1)} collective-permute-done((bf16[256,256]{0,1:T(8,128)(2,1)S(1)}, bf16[256,256]{0,1:T(8,128)(2,1)S(1)}, u32[]{:S(2)}, u32[]{:S(2)}) %collective-permute-start) | collective-permute-done | bytes 131104 | tf_op jit(solution)/shard_map/while/body/eval_jaxpr/ppermute | solution.py:19
  228.5 6.6 %collective-permute-done = bf16[256,256]{0,1:T(8,128)(2,1)S(1)} collective-permute-done((bf16[256,256]{0,1:T(8,128)(2,1)S(1)}, bf16[256,256]{0,1:T(8,128)(2,1)S(1)}, u32[]{:S(2)}, u32[]{:S(2)}) %collective-permute-start) | collective-permute-done | bytes 131104 | tf_op jit(solution)/shard_map/while/body/eval_jaxpr/ppermute | solution.py:19
  247.1 6.6 %collective-permute-done = bf16[256,256]{0,1:T(8,128)(2,1)S(1)} collective-permute-done((bf16[256,256]{0,1:T(8,128)(2,1)S(1)}, bf16[256,256]{0,1:T(8,128)(2,1)S(1)}, u32[]{:S(2)}, u32[]{:S(2)}) %collective-permute-start) | collective-permute-done | bytes 131104 | tf_op jit(solution)/shard_map/while/body/eval_jaxpr/ppermute | solution.py:19
  265.8 6.6 %collective-permute-done = bf16[256,256]{0,1:T(8,128)(2,1)S(1)} collective-permute-done((bf16[256,256]{0,1:T(8,128)(2,1)S(1)}, bf16[256,256]{0,1:T(8,128)(2,1)S(1)}, u32[]{:S(2)}, u32[]{:S(2)}) %collective-permute-start) | collective-permute-done | bytes 131104 | tf_op jit(solution)/shard_map/while/body/eval_jaxpr/ppermute | solution.py:19
  284.4 6.6 %collective-permute-done = bf16[256,256]{0,1:T(8,128)(2,1)S(1)} collective-permute-done((bf16[256,256]{0,1:T(8,128)(2,1)S(1)}, bf16[256,256]{0,1:T(8,128)(2,1)S(1)}, u32[]{:S(2)}, u32[]{:S(2)}) %collective-permute-start) | collective-permute-done | bytes 131104 | tf_op jit(solution)/shard_map/while/body/eval_jaxpr/ppermute | solution.py:19
  303.1 6.6 %collective-permute-done = bf16[256,256]{0,1:T(8,128)(2,1)S(1)} collective-permute-done((bf16[256,256]{0,1:T(8,128)(2,1)S(1)}, bf16[256,256]{0,1:T(8,128)(2,1)S(1)}, u32[]{:S(2)}, u32[]{:S(2)}) %collective-permute-start) | collective-permute-done | bytes 131104 | tf_op jit(solution)/shard_map/while/body/eval_jaxpr/ppermute | solution.py:19
  322.5 4.6 convolution_convert_fusion
  328.9 16.3 %reduce-scatter.2.cloned.1.call-done = bf16[256,1024]{1,0:T(8,128)(2,1)} async-done(((bf16[256,2048]{1,0:T(8,128)(2,1)}), bf16[256,1024]{1,0:T(8,128)(2,1)}) %reduce-scatter.2.cloned.1.call-update) | async-done | bytes 524304 | tf_op jit(solution)/shard_map/reduce_scatter | solution.py:172
  347.8 78.9 %all-gather.2.cloned.1.call-done = f32[32,32,2048]{2,1,0:T(8,128)} async-done(((f32[1,32,2048]{2,1,0:T(8,128)}), f32[32,32,2048]{2,1,0:T(8,128)}) %all-gather.2.cloned.1.call-update) | async-done | bytes 8388624 | tf_op jit(solution)/shard_map/all_gather | solution.py:185
  426.6 3.8 reduce_sum.120
  430.7 3.6 convolution_reduce_fusion
  435.1 39.2 %pmax.7 = f32[32]{0:T(128)} all-reduce(f32[32]{0:T(128)S(1)} %convolution_reduce_fusion), channel_id=1, replica_groups=mesh['seq'=16,'mp'=2] {'seq','mp'}, use_global_device_ids=true, to_apply=%region_19.20 | all-reduce | flops 32 | bytes 256 | tf_op jit(solution)/shard_map/pmax | solution.py:189
  (478 shorter events, 214.3 us)
Async XLA Ops:
  7.2 338.0 %reduce-scatter.2.cloned.1.call-start = ((), (), s32[]{:S(2)}) async-start(), calls=%async_computation.1 | async-start | bytes 1572864 | tf_op jit(solution)/shard_map/reduce_scatter | solution.py:172
  40.4 8.1 %collective-permute-start = (bf16[256,256]{0,1:T(8,128)(2,1)S(1)}, bf16[256,256]{0,1:T(8,128)(2,1)S(1)}, u32[]{:S(2)}, u32[]{:S(2)}) collective-permute-start(bf16[256,256]{0,1:T(8,128)(2,1)S(1)} %get-tuple-element.568), channel_id=1, source_target_pairs={{30,0},{0,2},{2,4},{4,6},{6,8},{8,10},{10,12},{12,14},{14,16},{16,... | collective-permute-start | bytes 393224 | tf_op jit(solution)/shard_map/while/body/eval_jaxpr/ppermute | solution.py:19
  40.9 10.4 %collective-permute-start.1 = (bf16[4,128,256]{1,0,2:T(4,128)(2,1)S(1)}, bf16[4,128,256]{1,0,2:T(4,128)(2,1)S(1)}, u32[]{:S(2)}, u32[]{:S(2)}) collective-permute-start(bf16[4,128,256]{1,0,2:T(4,128)(2,1)S(1)} %get-tuple-element.567), channel_id=1, source_target_pairs={{30,0},{0,2},{2,4},{4,6},{6,8},{8,10},{10,12},{12,14},{14,16},{16,... | collective-permute-start | bytes 786440 | tf_op jit(solution)/shard_map/while/body/eval_jaxpr/ppermute | solution.py:19
  60.0 7.1 %collective-permute-start = (bf16[256,256]{0,1:T(8,128)(2,1)S(1)}, bf16[256,256]{0,1:T(8,128)(2,1)S(1)}, u32[]{:S(2)}, u32[]{:S(2)}) collective-permute-start(bf16[256,256]{0,1:T(8,128)(2,1)S(1)} %get-tuple-element.568), channel_id=1, source_target_pairs={{30,0},{0,2},{2,4},{4,6},{6,8},{8,10},{10,12},{12,14},{14,16},{16,... | collective-permute-start | bytes 393224 | tf_op jit(solution)/shard_map/while/body/eval_jaxpr/ppermute | solution.py:19
  60.1 9.9 %collective-permute-start.1 = (bf16[4,128,256]{1,0,2:T(4,128)(2,1)S(1)}, bf16[4,128,256]{1,0,2:T(4,128)(2,1)S(1)}, u32[]{:S(2)}, u32[]{:S(2)}) collective-permute-start(bf16[4,128,256]{1,0,2:T(4,128)(2,1)S(1)} %get-tuple-element.567), channel_id=1, source_target_pairs={{30,0},{0,2},{2,4},{4,6},{6,8},{8,10},{10,12},{12,14},{14,16},{16,... | collective-permute-start | bytes 786440 | tf_op jit(solution)/shard_map/while/body/eval_jaxpr/ppermute | solution.py:19
  78.7 7.1 %collective-permute-start = (bf16[256,256]{0,1:T(8,128)(2,1)S(1)}, bf16[256,256]{0,1:T(8,128)(2,1)S(1)}, u32[]{:S(2)}, u32[]{:S(2)}) collective-permute-start(bf16[256,256]{0,1:T(8,128)(2,1)S(1)} %get-tuple-element.568), channel_id=1, source_target_pairs={{30,0},{0,2},{2,4},{4,6},{6,8},{8,10},{10,12},{12,14},{14,16},{16,... | collective-permute-start | bytes 393224 | tf_op jit(solution)/shard_map/while/body/eval_jaxpr/ppermute | solution.py:19
  78.7 9.9 %collective-permute-start.1 = (bf16[4,128,256]{1,0,2:T(4,128)(2,1)S(1)}, bf16[4,128,256]{1,0,2:T(4,128)(2,1)S(1)}, u32[]{:S(2)}, u32[]{:S(2)}) collective-permute-start(bf16[4,128,256]{1,0,2:T(4,128)(2,1)S(1)} %get-tuple-element.567), channel_id=1, source_target_pairs={{30,0},{0,2},{2,4},{4,6},{6,8},{8,10},{10,12},{12,14},{14,16},{16,... | collective-permute-start | bytes 786440 | tf_op jit(solution)/shard_map/while/body/eval_jaxpr/ppermute | solution.py:19
  97.3 7.1 %collective-permute-start = (bf16[256,256]{0,1:T(8,128)(2,1)S(1)}, bf16[256,256]{0,1:T(8,128)(2,1)S(1)}, u32[]{:S(2)}, u32[]{:S(2)}) collective-permute-start(bf16[256,256]{0,1:T(8,128)(2,1)S(1)} %get-tuple-element.568), channel_id=1, source_target_pairs={{30,0},{0,2},{2,4},{4,6},{6,8},{8,10},{10,12},{12,14},{14,16},{16,... | collective-permute-start | bytes 393224 | tf_op jit(solution)/shard_map/while/body/eval_jaxpr/ppermute | solution.py:19
  97.4 9.9 %collective-permute-start.1 = (bf16[4,128,256]{1,0,2:T(4,128)(2,1)S(1)}, bf16[4,128,256]{1,0,2:T(4,128)(2,1)S(1)}, u32[]{:S(2)}, u32[]{:S(2)}) collective-permute-start(bf16[4,128,256]{1,0,2:T(4,128)(2,1)S(1)} %get-tuple-element.567), channel_id=1, source_target_pairs={{30,0},{0,2},{2,4},{4,6},{6,8},{8,10},{10,12},{12,14},{14,16},{16,... | collective-permute-start | bytes 786440 | tf_op jit(solution)/shard_map/while/body/eval_jaxpr/ppermute | solution.py:19
  116.1 9.9 %collective-permute-start.1 = (bf16[4,128,256]{1,0,2:T(4,128)(2,1)S(1)}, bf16[4,128,256]{1,0,2:T(4,128)(2,1)S(1)}, u32[]{:S(2)}, u32[]{:S(2)}) collective-permute-start(bf16[4,128,256]{1,0,2:T(4,128)(2,1)S(1)} %get-tuple-element.567), channel_id=1, source_target_pairs={{30,0},{0,2},{2,4},{4,6},{6,8},{8,10},{10,12},{12,14},{14,16},{16,... | collective-permute-start | bytes 786440 | tf_op jit(solution)/shard_map/while/body/eval_jaxpr/ppermute | solution.py:19
  134.7 9.9 %collective-permute-start.1 = (bf16[4,128,256]{1,0,2:T(4,128)(2,1)S(1)}, bf16[4,128,256]{1,0,2:T(4,128)(2,1)S(1)}, u32[]{:S(2)}, u32[]{:S(2)}) collective-permute-start(bf16[4,128,256]{1,0,2:T(4,128)(2,1)S(1)} %get-tuple-element.567), channel_id=1, source_target_pairs={{30,0},{0,2},{2,4},{4,6},{6,8},{8,10},{10,12},{12,14},{14,16},{16,... | collective-permute-start | bytes 786440 | tf_op jit(solution)/shard_map/while/body/eval_jaxpr/ppermute | solution.py:19
  153.3 7.1 %collective-permute-start = (bf16[256,256]{0,1:T(8,128)(2,1)S(1)}, bf16[256,256]{0,1:T(8,128)(2,1)S(1)}, u32[]{:S(2)}, u32[]{:S(2)}) collective-permute-start(bf16[256,256]{0,1:T(8,128)(2,1)S(1)} %get-tuple-element.568), channel_id=1, source_target_pairs={{30,0},{0,2},{2,4},{4,6},{6,8},{8,10},{10,12},{12,14},{14,16},{16,... | collective-permute-start | bytes 393224 | tf_op jit(solution)/shard_map/while/body/eval_jaxpr/ppermute | solution.py:19
  153.4 9.9 %collective-permute-start.1 = (bf16[4,128,256]{1,0,2:T(4,128)(2,1)S(1)}, bf16[4,128,256]{1,0,2:T(4,128)(2,1)S(1)}, u32[]{:S(2)}, u32[]{:S(2)}) collective-permute-start(bf16[4,128,256]{1,0,2:T(4,128)(2,1)S(1)} %get-tuple-element.567), channel_id=1, source_target_pairs={{30,0},{0,2},{2,4},{4,6},{6,8},{8,10},{10,12},{12,14},{14,16},{16,... | collective-permute-start | bytes 786440 | tf_op jit(solution)/shard_map/while/body/eval_jaxpr/ppermute | solution.py:19
  172.0 9.9 %collective-permute-start.1 = (bf16[4,128,256]{1,0,2:T(4,128)(2,1)S(1)}, bf16[4,128,256]{1,0,2:T(4,128)(2,1)S(1)}, u32[]{:S(2)}, u32[]{:S(2)}) collective-permute-start(bf16[4,128,256]{1,0,2:T(4,128)(2,1)S(1)} %get-tuple-element.567), channel_id=1, source_target_pairs={{30,0},{0,2},{2,4},{4,6},{6,8},{8,10},{10,12},{12,14},{14,16},{16,... | collective-permute-start | bytes 786440 | tf_op jit(solution)/shard_map/while/body/eval_jaxpr/ppermute | solution.py:19
  190.6 7.1 %collective-permute-start = (bf16[256,256]{0,1:T(8,128)(2,1)S(1)}, bf16[256,256]{0,1:T(8,128)(2,1)S(1)}, u32[]{:S(2)}, u32[]{:S(2)}) collective-permute-start(bf16[256,256]{0,1:T(8,128)(2,1)S(1)} %get-tuple-element.568), channel_id=1, source_target_pairs={{30,0},{0,2},{2,4},{4,6},{6,8},{8,10},{10,12},{12,14},{14,16},{16,... | collective-permute-start | bytes 393224 | tf_op jit(solution)/shard_map/while/body/eval_jaxpr/ppermute | solution.py:19
  190.7 9.9 %collective-permute-start.1 = (bf16[4,128,256]{1,0,2:T(4,128)(2,1)S(1)}, bf16[4,128,256]{1,0,2:T(4,128)(2,1)S(1)}, u32[]{:S(2)}, u32[]{:S(2)}) collective-permute-start(bf16[4,128,256]{1,0,2:T(4,128)(2,1)S(1)} %get-tuple-element.567), channel_id=1, source_target_pairs={{30,0},{0,2},{2,4},{4,6},{6,8},{8,10},{10,12},{12,14},{14,16},{16,... | collective-permute-start | bytes 786440 | tf_op jit(solution)/shard_map/while/body/eval_jaxpr/ppermute | solution.py:19
  209.3 9.9 %collective-permute-start.1 = (bf16[4,128,256]{1,0,2:T(4,128)(2,1)S(1)}, bf16[4,128,256]{1,0,2:T(4,128)(2,1)S(1)}, u32[]{:S(2)}, u32[]{:S(2)}) collective-permute-start(bf16[4,128,256]{1,0,2:T(4,128)(2,1)S(1)} %get-tuple-element.567), channel_id=1, source_target_pairs={{30,0},{0,2},{2,4},{4,6},{6,8},{8,10},{10,12},{12,14},{14,16},{16,... | collective-permute-start | bytes 786440 | tf_op jit(solution)/shard_map/while/body/eval_jaxpr/ppermute | solution.py:19
  228.0 9.9 %collective-permute-start.1 = (bf16[4,128,256]{1,0,2:T(4,128)(2,1)S(1)}, bf16[4,128,256]{1,0,2:T(4,128)(2,1)S(1)}, u32[]{:S(2)}, u32[]{:S(2)}) collective-permute-start(bf16[4,128,256]{1,0,2:T(4,128)(2,1)S(1)} %get-tuple-element.567), channel_id=1, source_target_pairs={{30,0},{0,2},{2,4},{4,6},{6,8},{8,10},{10,12},{12,14},{14,16},{16,... | collective-permute-start | bytes 786440 | tf_op jit(solution)/shard_map/while/body/eval_jaxpr/ppermute | solution.py:19
  246.6 9.9 %collective-permute-start.1 = (bf16[4,128,256]{1,0,2:T(4,128)(2,1)S(1)}, bf16[4,128,256]{1,0,2:T(4,128)(2,1)S(1)}, u32[]{:S(2)}, u32[]{:S(2)}) collective-permute-start(bf16[4,128,256]{1,0,2:T(4,128)(2,1)S(1)} %get-tuple-element.567), channel_id=1, source_target_pairs={{30,0},{0,2},{2,4},{4,6},{6,8},{8,10},{10,12},{12,14},{14,16},{16,... | collective-permute-start | bytes 786440 | tf_op jit(solution)/shard_map/while/body/eval_jaxpr/ppermute | solution.py:19
  265.3 9.9 %collective-permute-start.1 = (bf16[4,128,256]{1,0,2:T(4,128)(2,1)S(1)}, bf16[4,128,256]{1,0,2:T(4,128)(2,1)S(1)}, u32[]{:S(2)}, u32[]{:S(2)}) collective-permute-start(bf16[4,128,256]{1,0,2:T(4,128)(2,1)S(1)} %get-tuple-element.567), channel_id=1, source_target_pairs={{30,0},{0,2},{2,4},{4,6},{6,8},{8,10},{10,12},{12,14},{14,16},{16,... | collective-permute-start | bytes 786440 | tf_op jit(solution)/shard_map/while/body/eval_jaxpr/ppermute | solution.py:19
  283.9 7.1 %collective-permute-start = (bf16[256,256]{0,1:T(8,128)(2,1)S(1)}, bf16[256,256]{0,1:T(8,128)(2,1)S(1)}, u32[]{:S(2)}, u32[]{:S(2)}) collective-permute-start(bf16[256,256]{0,1:T(8,128)(2,1)S(1)} %get-tuple-element.568), channel_id=1, source_target_pairs={{30,0},{0,2},{2,4},{4,6},{6,8},{8,10},{10,12},{12,14},{14,16},{16,... | collective-permute-start | bytes 393224 | tf_op jit(solution)/shard_map/while/body/eval_jaxpr/ppermute | solution.py:19
  283.9 9.9 %collective-permute-start.1 = (bf16[4,128,256]{1,0,2:T(4,128)(2,1)S(1)}, bf16[4,128,256]{1,0,2:T(4,128)(2,1)S(1)}, u32[]{:S(2)}, u32[]{:S(2)}) collective-permute-start(bf16[4,128,256]{1,0,2:T(4,128)(2,1)S(1)} %get-tuple-element.567), channel_id=1, source_target_pairs={{30,0},{0,2},{2,4},{4,6},{6,8},{8,10},{10,12},{12,14},{14,16},{16,... | collective-permute-start | bytes 786440 | tf_op jit(solution)/shard_map/while/body/eval_jaxpr/ppermute | solution.py:19
  302.6 9.9 %collective-permute-start.1 = (bf16[4,128,256]{1,0,2:T(4,128)(2,1)S(1)}, bf16[4,128,256]{1,0,2:T(4,128)(2,1)S(1)}, u32[]{:S(2)}, u32[]{:S(2)}) collective-permute-start(bf16[4,128,256]{1,0,2:T(4,128)(2,1)S(1)} %get-tuple-element.567), channel_id=1, source_target_pairs={{30,0},{0,2},{2,4},{4,6},{6,8},{8,10},{10,12},{12,14},{14,16},{16,... | collective-permute-start | bytes 786440 | tf_op jit(solution)/shard_map/while/body/eval_jaxpr/ppermute | solution.py:19
  327.1 99.6 %all-gather.2.cloned.1.call-start = ((), (), s32[]{:S(2)}) async-start(), calls=%async_computation.2 | async-start | bytes 8650752 | tf_op jit(solution)/shard_map/all_gather | solution.py:185
  (53 other events, 334.9 us)
Sparse Core Ops, SparseCore 0:
  327.2 17.9 reduce-scatter.1
  349.2 77.3 all-gather.1
